TPU v7x, 256 devices: a whole 4x4x8 slice. The times are simulated.
256 devices in a mesh: dp: 64 (over y, z, core), vocab: 4 (over x).
Axes of the slice: x: 4, y: 4, z: 8, core: 2. Of those that a mesh axis runs over, the one named last changes fastest.
Arguments:
- hidden_rows: bfloat16 [16384, 5120], P('dp'), may hold values from -300 to 300, as said below
- plan_lengths: int32 [64], replicated, may hold values from 1 to 256, 8192 in all
- shard_of_class: int32 [64], replicated, may hold values from 0 to 63, each once
- head_weight: bfloat16 [5120, 3072], P(None, 'vocab'), may hold values from -0.078125 to 0.078125
- teacher_logprobs: bfloat16 [8192, 3072], P('dp', 'vocab'), as said below
Outputs:
- row_grad: bfloat16 [16384, 5120], P('dp')
- row_kl: float32 [8192], P('dp')
Inputs may be any that keep to these rules, and one draw needn't show every extreme that they name: `plan_lengths`: the plan lengths sum to 8192 and the longest is exactly 256. `shard_of_class`: each shard is named once. `hidden_rows`: unused slots hold finite values. `teacher_logprobs`: each row is a log-softmax over the 3072 entries, rounded to bfloat16.
All inputs are finite; a program needn't handle non-finite values.
Results may differ from a plain program's by a relative error of at most 0.0046.
Values may be sent and summed in bfloat16 or wider, within the bound.
No kernel may reach another device: no remote copies, remote signals or barrier semaphores. Data moves between devices by JAX's collectives and lax.ppermute only.
A program may use at most 64 MiB of HBM per device.

v0:
```python
import jax
import jax.numpy as jnp
from jax import lax
from jax.sharding import PartitionSpec as P

loss_scale = 64.0


def divergence(row_block, teacher_block, live_rows, weight):
    logits = jnp.dot(row_block, weight, preferred_element_type=jnp.float32)
    log_teacher = teacher_block.astype(jnp.float32)
    teacher_prob = jnp.exp(log_teacher)
    own_top = jnp.max(logits, axis=1)
    own_mass = jnp.sum(teacher_prob, axis=1)
    own_cross = jnp.sum(teacher_prob * (log_teacher - logits), axis=1)
    row_top = lax.pmax(own_top, "vocab")
    own_total = jnp.sum(jnp.exp(logits - row_top[:, None]), axis=1)
    exp_total, prob_total, cross_term = lax.psum((own_total, own_mass, own_cross), "vocab")
    log_total = row_top + jnp.log(exp_total)
    row_div = (cross_term + prob_total * log_total) * live_rows
    grad_logits = (
        loss_scale
        * (prob_total[:, None] * jnp.exp(logits - log_total[:, None]) - teacher_prob)
        * live_rows[:, None]
    ).astype(jnp.bfloat16)
    partial_grad = lax.dot_general(
        grad_logits, weight, (((1,), (1,)), ((), ())), preferred_element_type=jnp.float32
    )
    hidden_grad = lax.psum(partial_grad, "vocab").astype(jnp.bfloat16)
    return (hidden_grad, row_div)


def body(hidden_rows, plan_lengths, shard_of_class, head_weight, teacher_logprobs):
    shards = lax.axis_size("dp")
    myself = lax.axis_index("dp")
    source_slots = hidden_rows.shape[0]
    feature_width = hidden_rows.shape[1]
    slot_depth = source_slots // shards
    balanced = teacher_logprobs.shape[0]
    offsets = jnp.cumsum(plan_lengths) - plan_lengths
    classes = jnp.arange(shards, dtype=jnp.int32)
    inverse = jnp.sum(
        jnp.where(shard_of_class[None, :] == classes[:, None], classes[None, :], 0), axis=1
    )
    own_offset = offsets[myself]
    column_of = (inverse - own_offset) % shards
    shard_at = shard_of_class[(own_offset + classes) % shards]
    rank_rows = jnp.arange(slot_depth, dtype=jnp.int32)[:, None]
    recv_row = rank_rows * shards + ((inverse[myself] - offsets) % shards)[None, :]
    recv_live = recv_row < plan_lengths[None, :]
    recv_slot = jnp.where(recv_live, (offsets[None, :] + recv_row) // shards, balanced)
    safe_slot = jnp.minimum(recv_slot, balanced - 1).reshape(-1)
    outgoing = jnp.take(hidden_rows.reshape(slot_depth, shards, feature_width), column_of, axis=1)
    arriving = lax.all_to_all(outgoing, "dp", split_axis=1, concat_axis=1, tiled=True)
    flattened = arriving.reshape(slot_depth * shards, feature_width)
    live_rows = recv_live.reshape(-1).astype(jnp.float32)
    teacher_slots = jnp.take(teacher_logprobs, safe_slot, axis=0)
    returning, row_div = divergence(flattened, teacher_slots, live_rows, head_weight)
    row_kl = jnp.zeros((balanced,), jnp.float32).at[recv_slot.reshape(-1)].add(row_div, mode="drop")
    share_width = returning.shape[1]
    returned = lax.all_to_all(
        returning.reshape(slot_depth, shards, share_width),
        "dp",
        split_axis=1,
        concat_axis=1,
        tiled=True,
    )
    grad_share = jnp.take(returned, shard_at, axis=1).reshape(source_slots, share_width)
    return (grad_share, row_kl)


def solution(mesh):
    return jax.shard_map(
        body,
        mesh=mesh,
        in_specs=(P("dp", None), P(), P(), P(None, "vocab"), P("dp", "vocab")),
        out_specs=(P("dp", None), P("dp")),
        check_vma=False,
    )
```

profile of v0, /device:TPU:1, one launch (start us, length us, event | category | flops | bytes accessed | tf_op | source)
XLA Modules:
  0.0 298.8 jit_solution(14799237197427120690)
XLA Ops:
  0.6 0.8 select_reduce_fusion
  1.5 0.8 copy.15
  3.0 1.3 and_select_fusion.4
  5.6 3.8 %copy.16 = bf16[4,64,5120]{2,0,1:T(4,128)(2,1)S(1)} copy(bf16[4,64,5120]{2,1,0:T(8,128)(2,1)} %bitcast.18) | data formatting | bytes 5242880 | tf_op jit(solution)/shard_map/reshape | solution.py:53
  9.3 4.2 %gather_fusion.2 = bf16[64,4,5120]{2,1,0:T(4,128)(2,1)} fusion(bf16[4,64,5120]{2,0,1:T(4,128)(2,1)S(1)} %copy.16, s32[1024]{0:T(1024)S(1)} %pad_clamp_fusion.1), kind=kCustom, calls=%fused_computation.clone | custom fusion | bytes 5243136 | tf_op jit(solution)/shard_map/jit(_take)/gather | solution.py:53
  13.5 4.5 %select_bitcast_fusion.1 = bf16[4,64,5120]{2,0,1:T(4,128)(2,1)} fusion(bf16[64,4,5120]{2,1,0:T(4,128)(2,1)} %gather_fusion.2, pred[64]{0:T(512)(128)(4,1)S(1)} %get-tuple-element.14), kind=kLoop, calls=%fused_computation.6 | loop fusion | flops 1310720 | bytes 5242944 | tf_op jit(solution)/shard_map/jit(_take)/select_n | solution.py:53
  18.0 13.3 %all-to-all-start = ((bf16[4,64,5120]{2,0,1:T(4,128)(2,1)}), bf16[4,64,5120]{2,0,1:T(4,128)(2,1)S(1)}, u32[]{:S(2)}, u32[]{:S(2)}) async-start(bf16[4,64,5120]{2,0,1:T(4,128)(2,1)} %select_bitcast_fusion.1), calls=%async_computation | async-start | bytes 5242880 | tf_op jit(solution)/shard_map/all_to_all | solution.py:54
  31.8 1.2 gather_fusion
  33.1 60.5 %all-to-all-done = bf16[4,64,5120]{2,0,1:T(4,128)(2,1)S(1)} async-done(((bf16[4,64,5120]{2,0,1:T(4,128)(2,1)}), bf16[4,64,5120]{2,0,1:T(4,128)(2,1)S(1)}, u32[]{:S(2)}, u32[]{:S(2)}) %all-to-all-start) | async-done | bytes 2621472 | tf_op jit(solution)/shard_map/all_to_all | solution.py:54
  93.5 0.8 copy.17
  94.3 5.5 %fusion.19 = (f32[256]{0:T(256)S(1)}, f32[256,768]{1,0:T(8,128)S(1)}) fusion(bf16[256,5120]{1,0:T(8,128)(2,1)S(1)} %bitcast.21, bf16[5120,768]{1,0:T(8,128)(2,1)} %param.10), kind=kOutput, calls=%fused_computation.66 | convolution fusion | flops 2013462272 | bytes 11273216 | tf_op jit(solution)/shard_map/dot_general | solution.py:10
  99.9 8.5 %pmax.7 = f32[256]{0:T(256)S(1)} all-reduce(f32[256]{0:T(256)S(1)} %get-tuple-element.16), channel_id=1, replica_groups=mesh['dp'=64,'vocab'=4] {'vocab'}, use_global_device_ids=true, to_apply=%region_5.7 | all-reduce | flops 256 | bytes 2048 | tf_op jit(solution)/shard_map/pmax | solution.py:16
  108.9 6.2 %all-reduce.1 = (f32[256]{0:T(256)S(1)}, f32[256]{0:T(256)S(1)}) all-reduce(f32[256]{0:T(256)S(1)} %get-tuple-element.4, f32[256]{0:T(256)S(1)} %get-tuple-element.5), channel_id=1, replica_groups=mesh['dp'=64,'vocab'=4] {'vocab'}, use_global_device_ids=true, to_apply=%region_7.9 | all-reduce | flops 512 | bytes 4096 | tf_op jit(solution)/shard_map/psum | solution.py:18
  115.1 8.0 %fusion.6 = f32[256,5120]{1,0:T(8,128)} fusion(bf16[5120,768]{1,0:T(8,128)(2,1)} %param.10, f32[256,768]{1,0:T(8,128)S(1)} %get-tuple-element.17, f32[256]{0:T(256)S(1)} %broadcast_select_fusion.1, f32[256]{0:T(256)S(1)} %log_add_fusion, f32[256]{0:T(256)S(1)} %get-tuple-element.9, bf16[256,768]{1,0:T(8,128)(2,1)S(1)} %gather_fusion, ...), kind=kOutput, calls=%fused_computation.16 | convolution fusion | flops 2014642176 | bytes 14290176 | tf_op jit(solution)/shard_map/dot_general | solution.py:26
  123.1 89.4 %all-reduce.3 = (bf16[256,5120]{1,0:T(8,128)(2,1)S(1)}, f32[256]{0:T(256)S(1)}) all-reduce(f32[256,5120]{1,0:T(8,128)} %fusion.6, f32[256]{0:T(256)S(1)} %get-tuple-element.3), channel_id=1, replica_groups=mesh['dp'=64,'vocab'=4] {'vocab'}, use_global_device_ids=true, to_apply=%region_8.10 | all-reduce | flops 1310976 | bytes 7866368 | tf_op jit(solution)/shard_map/psum | solution.py:29
  212.5 3.5 %copy.18 = bf16[4,64,5120]{2,0,1:T(4,128)(2,1)} copy(bf16[4,64,5120]{2,1,0:T(8,128)(2,1)S(1)} %bitcast.20) | data formatting | bytes 5242880 | tf_op jit(solution)/shard_map/reshape | solution.py:62
  216.0 11.2 %all-to-all-start.1 = ((bf16[4,64,5120]{2,0,1:T(4,128)(2,1)}), bf16[4,64,5120]{2,0,1:T(4,128)(2,1)S(1)}, u32[]{:S(2)}, u32[]{:S(2)}) async-start(bf16[4,64,5120]{2,0,1:T(4,128)(2,1)} %copy.18), calls=%async_computation.1 | async-start | bytes 5242880 | tf_op jit(solution)/shard_map/all_to_all | solution.py:61
  227.1 0.7 fusion.15
  227.8 0.8 gather_fusion.1
  228.6 2.8 scatter_custom_fusion
  231.5 57.9 %all-to-all-done.1 = bf16[4,64,5120]{2,0,1:T(4,128)(2,1)S(1)} async-done(((bf16[4,64,5120]{2,0,1:T(4,128)(2,1)}), bf16[4,64,5120]{2,0,1:T(4,128)(2,1)S(1)}, u32[]{:S(2)}, u32[]{:S(2)}) %all-to-all-start.1) | async-done | bytes 2621472 | tf_op jit(solution)/shard_map/all_to_all | solution.py:61
  289.4 4.2 %gather_fusion.3 = bf16[64,4,5120]{2,1,0:T(4,128)(2,1)} fusion(bf16[4,64,5120]{2,0,1:T(4,128)(2,1)S(1)} %all-to-all-done.1, s32[1024]{0:T(1024)S(1)} %pad_clamp_fusion), kind=kCustom, calls=%fused_computation.1.clone | custom fusion | bytes 5243136 | tf_op jit(solution)/shard_map/jit(_take)/gather | solution.py:68
  293.5 3.0 %select_bitcast_fusion = bf16[4,64,5120]{2,0,1:T(4,128)(2,1)S(1)} fusion(bf16[64,4,5120]{2,1,0:T(4,128)(2,1)} %gather_fusion.3, pred[64]{0:T(512)(128)(4,1)S(1)} %compare_and_fusion), kind=kLoop, calls=%fused_computation.5 | loop fusion | flops 1310720 | bytes 5242944 | tf_op jit(solution)/shard_map/jit(_take)/select_n | solution.py:68
  296.5 2.3 copy.19
  (31 shorter events, 3.2 us)
Async XLA Ops:
  0.6 31.2 %copy-start = (bf16[128,768]{1,0:T(8,128)(2,1)S(1)}, bf16[128,768]{1,0:T(8,128)(2,1)}, u32[]{:S(2)}) copy-start(bf16[128,768]{1,0:T(8,128)(2,1)} %param.11) | copy-start | bytes 589828
  18.0 13.5 %copy-start.2 = (s32[64]{0:T(128)S(1)}, s32[64]{0:T(128)}, u32[]{:S(2)}) copy-start(s32[64]{0:T(128)} %param.8) | copy-start | bytes 772
  18.0 75.5 %all-to-all-start = ((bf16[4,64,5120]{2,0,1:T(4,128)(2,1)}), bf16[4,64,5120]{2,0,1:T(4,128)(2,1)S(1)}, u32[]{:S(2)}, u32[]{:S(2)}) async-start(bf16[4,64,5120]{2,0,1:T(4,128)(2,1)} %select_bitcast_fusion.1), calls=%async_computation | async-start | bytes 5242880 | tf_op jit(solution)/shard_map/all_to_all | solution.py:54
  216.0 11.8 %copy-start.1 = (s32[64]{0:T(128)S(1)}, s32[64]{0:T(128)}, u32[]{:S(2)}) copy-start(s32[64]{0:T(128)} %param.9) | copy-start | bytes 772
  216.0 73.4 %all-to-all-start.1 = ((bf16[4,64,5120]{2,0,1:T(4,128)(2,1)}), bf16[4,64,5120]{2,0,1:T(4,128)(2,1)S(1)}, u32[]{:S(2)}, u32[]{:S(2)}) async-start(bf16[4,64,5120]{2,0,1:T(4,128)(2,1)} %copy.18), calls=%async_computation.1 | async-start | bytes 5242880 | tf_op jit(solution)/shard_map/all_to_all | solution.py:61
where the time goes:
time: 299 us
  waiting for transfers between devices  118 us (39%)
  blocking collectives  104 us (35%)
  starting transfers between devices  24.4 us (8%)
  local copies, waits for them, and re-layouts  22.9 us (8%)
  other arithmetic  14.8 us (5%)
  matrix products  13.5 us (5%)
    psum x1, blocking collectives, divergence(): hidden_grad = lax.psum(partial_grad, 'vocab').astype(jnp.bfloat16)  89.4 us
    all_to_all x1, waiting for transfers between devices, body(): lax.all_to_all(outgoing, 'dp', split_axis=1, concat_axis=1, tiled=True)  60.5 us
    all_to_all x1, waiting for transfers between devices, body(): lax.all_to_all(returning.reshape(slot_depth, shards, share_width), 'dp',...  57.9 us
    all_to_all x1, starting transfers between devices, body(): lax.all_to_all(outgoing, 'dp', split_axis=1, concat_axis=1, tiled=True)  13.3 us
    all_to_all x1, starting transfers between devices, body(): lax.all_to_all(returning.reshape(slot_depth, shards, share_width), 'dp',...  11.2 us
    pmax x1, blocking collectives, divergence(): row_top = lax.pmax(own_top, 'vocab')  8.47 us
    dot_general x1, matrix products, divergence(): lax.dot_general(grad_logits, weight, (((1,), (1,)), ((), ())), preferred_...  7.99 us
    psum x1, blocking collectives, divergence(): lax.psum((own_total, own_mass, own_cross), 'vocab')  6.18 us
  transfers between devices with their start and end apart: 2, of which 2 were waited for; matrix products, arithmetic and copies ran while one was open for 2% of the time, Pallas kernels for 0%

commit v1 on v0

--- a/solution.py
+++ b/solution.py
@@ -2,6 +2,7 @@
 import jax.numpy as jnp
 from jax import lax
 from jax.sharding import PartitionSpec as P
+from jax.lax import all_gather
 
 loss_scale = 64.0
 
@@ -26,7 +27,7 @@
     partial_grad = lax.dot_general(
         grad_logits, weight, (((1,), (1,)), ((), ())), preferred_element_type=jnp.float32
     )
-    hidden_grad = lax.psum(partial_grad, "vocab").astype(jnp.bfloat16)
+    hidden_grad = jnp.sum(all_gather(partial_grad, axis_name="vocab"), 0).astype(jnp.bfloat16)
     return (hidden_grad, row_div)
 
 

time: 299 us -> 423 us (1.41)
  waiting for transfers between devices: 118 us -> 310 us
  blocking collectives: 104 us -> 14.7 us
  between operations: 0.79 us -> 14.2 us
  other arithmetic: 14.8 us -> 23.8 us
    all_gather x0 -> x1, waiting for transfers between devices: none -> 191 us  [divergence(): all_gather(partial_grad, axis_name='vocab')]
    psum x1 -> x0, blocking collectives: 89.4 us -> none  [divergence(): hidden_grad = lax.psum(partial_grad, 'vocab').astype(jnp.bfloat16)]
    reduce_sum x0 -> x1, other arithmetic: none -> 8.99 us  [divergence(): jnp.sum(all_gather(partial_grad, axis_name='vocab'), 0).astype(jnp.bfloat16)]
  transfers between devices with their start and end apart: 2 -> 3, of which waited for: 2 -> 3; matrix products, arithmetic and copies ran while one was open for 2% -> 1% of each run, Pallas kernels for 0% -> 0%
where the time goes in v1:
time: 423 us
  waiting for transfers between devices  310 us (73%)
  starting transfers between devices  24.3 us (6%)
  other arithmetic  23.8 us (6%)
  local copies, waits for them, and re-layouts  22.9 us (5%)
  blocking collectives  14.7 us (3%)
  between operations  14.2 us (3%)
  matrix products  13.5 us (3%)
    all_gather x1, waiting for transfers between devices, divergence(): all_gather(partial_grad, axis_name='vocab')  191 us
    all_to_all x1, waiting for transfers between devices, body(): lax.all_to_all(outgoing, 'dp', split_axis=1, concat_axis=1, tiled=True)  60.4 us
    all_to_all x1, waiting for transfers between devices, body(): lax.all_to_all(returning.reshape(slot_depth, shards, share_width), 'dp',...  57.9 us
    all_to_all x1, starting transfers between devices, body(): lax.all_to_all(outgoing, 'dp', split_axis=1, concat_axis=1, tiled=True)  13.3 us
    all_to_all x1, starting transfers between devices, body(): lax.all_to_all(returning.reshape(slot_depth, shards, share_width), 'dp',...  11 us
    reduce_sum x1, other arithmetic, divergence(): jnp.sum(all_gather(partial_grad, axis_name='vocab'), 0).astype(jnp.bfloat16)  8.99 us
    pmax x1, blocking collectives, divergence(): row_top = lax.pmax(own_top, 'vocab')  8.47 us
  transfers between devices with their start and end apart: 3, of which 3 were waited for; matrix products, arithmetic and copies ran while one was open for 1% of the time, Pallas kernels for 0%

profile of v1, /device:TPU:1, one launch (start us, length us, event | category | flops | bytes accessed | tf_op | source)
XLA Modules:
  0.0 422.9 jit_solution(1654084126162623826)
XLA Ops:
  7.2 0.8 select_reduce_fusion
  8.0 0.8 copy.14
  9.5 1.3 and_select_fusion.4
  12.1 3.8 copy.15
  15.9 4.2 gather_fusion.2
  20.0 4.5 %select_bitcast_fusion.1 = bf16[4,64,5120]{2,0,1:T(4,128)(2,1)} fusion(bf16[64,4,5120]{2,1,0:T(4,128)(2,1)} %gather_fusion.2, pred[64]{0:T(512)(128)(4,1)S(1)} %get-tuple-element.15), kind=kLoop, calls=%fused_computation.6 | loop fusion | flops 1310720 | bytes 5242944 | tf_op jit(solution)/shard_map/jit(_take)/select_n | solution.py:54
  24.5 13.3 %all-to-all-start = ((bf16[4,64,5120]{2,0,1:T(4,128)(2,1)}), bf16[4,64,5120]{2,0,1:T(4,128)(2,1)S(1)}, u32[]{:S(2)}, u32[]{:S(2)}) async-start(bf16[4,64,5120]{2,0,1:T(4,128)(2,1)} %select_bitcast_fusion.1), calls=%async_computation | async-start | bytes 5242880 | tf_op jit(solution)/shard_map/all_to_all | solution.py:55
  38.4 1.2 gather_fusion
  39.6 60.4 %all-to-all-done = bf16[4,64,5120]{2,0,1:T(4,128)(2,1)S(1)} async-done(((bf16[4,64,5120]{2,0,1:T(4,128)(2,1)}), bf16[4,64,5120]{2,0,1:T(4,128)(2,1)S(1)}, u32[]{:S(2)}, u32[]{:S(2)}) %all-to-all-start) | async-done | bytes 2621472 | tf_op jit(solution)/shard_map/all_to_all | solution.py:55
  100.1 0.8 copy.16
  100.8 5.5 %fusion.19 = (f32[256]{0:T(256)S(1)}, f32[256,768]{1,0:T(8,128)S(1)}) fusion(bf16[256,5120]{1,0:T(8,128)(2,1)S(1)} %bitcast.23, bf16[5120,768]{1,0:T(8,128)(2,1)} %param.10), kind=kOutput, calls=%fused_computation.66 | convolution fusion | flops 2013462272 | bytes 11273216 | tf_op jit(solution)/shard_map/dot_general | solution.py:11
  106.4 8.5 %pmax.7 = f32[256]{0:T(256)S(1)} all-reduce(f32[256]{0:T(256)S(1)} %get-tuple-element.18), channel_id=1, replica_groups=mesh['dp'=64,'vocab'=4] {'vocab'}, use_global_device_ids=true, to_apply=%region_5.7 | all-reduce | flops 256 | bytes 2048 | tf_op jit(solution)/shard_map/pmax | solution.py:17
  115.4 6.2 %all-reduce = (f32[256]{0:T(256)S(1)}, f32[256]{0:T(256)S(1)}, f32[256]{0:T(256)S(1)}) all-reduce(f32[256]{0:T(256)S(1)} %get-tuple-element.4, f32[256]{0:T(256)S(1)} %get-tuple-element.5, f32[256]{0:T(256)S(1)} %get-tuple-element.3), channel_id=1, replica_groups=mesh['dp'=64,'vocab'=4] {'vocab'}, use_global_device_ids=true, to_apply=%region_7.9 | all-reduce | flops 768 | bytes 6144 | tf_op jit(solution)/shard_map/psum | solution.py:19
  121.6 8.0 %fusion.6 = f32[256,5120]{1,0:T(8,128)} fusion(bf16[5120,768]{1,0:T(8,128)(2,1)} %param.10, f32[256,768]{1,0:T(8,128)S(1)} %get-tuple-element.19, f32[256]{0:T(256)S(1)} %get-tuple-element.17, f32[256]{0:T(256)S(1)} %get-tuple-element.10, f32[256]{0:T(256)S(1)} %get-tuple-element.7, bf16[256,768]{1,0:T(8,128)(2,1)S(1)} %gather_fusion, ...), kind=kOutput, calls=%fused_computation.16 | convolution fusion | flops 2014642176 | bytes 14290176 | tf_op jit(solution)/shard_map/dot_general | solution.py:27
  129.7 191.2 %all-gather.3.cloned.1.call-done = f32[1024,5120]{1,0:T(8,128)} async-done(((f32[256,5120]{1,0:T(8,128)}), f32[1024,5120]{1,0:T(8,128)}) %all-gather.3.cloned.1.call-update) | async-done | bytes 20971536 | tf_op jit(solution)/shard_map/all_gather | solution.py:30
  320.8 9.0 %reduce_sum.48 = bf16[256,5120]{1,0:T(8,128)(2,1)S(1)} reduce(f32[4,256,5120]{2,1,0:T(8,128)} %bitcast.19, f32[]{:T(128)} %constant.86.clone.1), dimensions={0}, to_apply=%region_8.10 | reduce | flops 3932160 | bytes 23592964 | tf_op jit(solution)/shard_map/reduce_sum | solution.py:30
  329.8 3.5 copy.17
  333.3 11.0 %all-to-all-start.1 = ((bf16[4,64,5120]{2,0,1:T(4,128)(2,1)}), bf16[4,64,5120]{2,0,1:T(4,128)(2,1)S(1)}, u32[]{:S(2)}, u32[]{:S(2)}) async-start(bf16[4,64,5120]{2,0,1:T(4,128)(2,1)} %copy.17), calls=%async_computation.1 | async-start | bytes 5242880 | tf_op jit(solution)/shard_map/all_to_all | solution.py:62
  345.0 0.8 gather_fusion.1
  345.8 2.8 scatter_custom_fusion
  348.7 57.9 %all-to-all-done.1 = bf16[4,64,5120]{2,0,1:T(4,128)(2,1)S(1)} async-done(((bf16[4,64,5120]{2,0,1:T(4,128)(2,1)}), bf16[4,64,5120]{2,0,1:T(4,128)(2,1)S(1)}, u32[]{:S(2)}, u32[]{:S(2)}) %all-to-all-start.1) | async-done | bytes 2621472 | tf_op jit(solution)/shard_map/all_to_all | solution.py:62
  406.6 4.2 gather_fusion.3
  410.7 3.0 select_bitcast_fusion
  413.7 2.3 copy.18
  (32 shorter events, 3.9 us)
Async XLA Ops:
  7.2 31.3 %copy-start = (bf16[128,768]{1,0:T(8,128)(2,1)S(1)}, bf16[128,768]{1,0:T(8,128)(2,1)}, u32[]{:S(2)}) copy-start(bf16[128,768]{1,0:T(8,128)(2,1)} %param.11) | copy-start | bytes 589828
  24.5 13.6 %copy-start.2 = (s32[64]{0:T(128)S(1)}, s32[64]{0:T(128)}, u32[]{:S(2)}) copy-start(s32[64]{0:T(128)} %param.8) | copy-start | bytes 772
  24.5 75.5 %all-to-all-start = ((bf16[4,64,5120]{2,0,1:T(4,128)(2,1)}), bf16[4,64,5120]{2,0,1:T(4,128)(2,1)S(1)}, u32[]{:S(2)}, u32[]{:S(2)}) async-start(bf16[4,64,5120]{2,0,1:T(4,128)(2,1)} %select_bitcast_fusion.1), calls=%async_computation | async-start | bytes 5242880 | tf_op jit(solution)/shard_map/all_to_all | solution.py:55
  37.8 283.0 %all-gather.3.cloned.1.call-start = ((), (), s32[]{:S(2)}) async-start(), calls=%async_computation.2 | async-start | bytes 26214400 | tf_op jit(solution)/shard_map/all_gather | solution.py:30
  333.3 11.7 %copy-start.1 = (s32[64]{0:T(128)S(1)}, s32[64]{0:T(128)}, u32[]{:S(2)}) copy-start(s32[64]{0:T(128)} %param.9) | copy-start | bytes 772
  333.3 73.2 %all-to-all-start.1 = ((bf16[4,64,5120]{2,0,1:T(4,128)(2,1)}), bf16[4,64,5120]{2,0,1:T(4,128)(2,1)S(1)}, u32[]{:S(2)}, u32[]{:S(2)}) async-start(bf16[4,64,5120]{2,0,1:T(4,128)(2,1)} %copy.17), calls=%async_computation.1 | async-start | bytes 5242880 | tf_op jit(solution)/shard_map/all_to_all | solution.py:62
Sparse Core Ops, SparseCore 0:
  129.8 190.9 all-gather.2
